TPU v7x, 32 devices: a whole 2x2x4 slice. The times are simulated.
32 devices in a mesh: row: 8 (over y, x, core), col: 4 (over z).
Axes of the slice: x: 2, y: 2, z: 4, core: 2. Of those that a mesh axis runs over, the one named last changes fastest.
Arguments:
- tokens: bfloat16 [192, 8192], P('col', 'row'), may hold values from -6 to 6
- grad_out: bfloat16 [192, 8192], P('col', 'row'), may hold values from -6 to 6
- gate_weight: bfloat16 [8192, 14336], P('row', 'col'), may hold values from -0.0625 to 0.0625
- up_weight: bfloat16 [8192, 14336], P('row', 'col'), may hold values from -0.0625 to 0.0625
- down_weight: bfloat16 [14336, 8192], P('col', 'row'), may hold values from -0.046875 to 0.046875
Outputs:
- grad_tokens: bfloat16 [192, 8192], P('col', 'row')
- grad_gate_weight: bfloat16 [8192, 14336], P('row', 'col')
- grad_up_weight: bfloat16 [8192, 14336], P('row', 'col')
- grad_down_weight: bfloat16 [14336, 8192], P('col', 'row')
All inputs are finite; a program needn't handle non-finite values.
Results may differ from a plain program's by a relative error of at most 0.024.
Values may be sent and summed in bfloat16 or wider, within the bound.
No kernel may reach another device: no remote copies, remote signals or barrier semaphores. Data moves between devices by JAX's collectives and lax.ppermute only.
A program may use at most 128 MiB of HBM per device.

v0:
```python
import jax
import jax.numpy as jnp
from jax import lax
from jax.sharding import PartitionSpec as P


def contract_first(left, right):
    return lax.dot_general(
        left, right, (((0,), (0,)), ((), ())), preferred_element_type=jnp.float32
    )


def contract_last(left, right):
    return lax.dot_general(
        left, right, (((1,), (1,)), ((), ())), preferred_element_type=jnp.float32
    )


def gated_grads(gate_sum, up_sum, grad_hidden):
    sigmoid_gate = jax.nn.sigmoid(gate_sum)
    hidden = (gate_sum * sigmoid_gate * up_sum).astype(jnp.bfloat16)
    grad_up = (grad_hidden * gate_sum * sigmoid_gate).astype(jnp.bfloat16)
    grad_gate = (
        grad_hidden * up_sum * sigmoid_gate * (1.0 + gate_sum * (1.0 - sigmoid_gate))
    ).astype(jnp.bfloat16)
    return (hidden, grad_gate, grad_up)


def body(tokens, grad_out, gate_weight, up_weight, down_weight):
    tok_all, grad_all = (
        lax.all_gather(tokens, "col", axis=0, tiled=True),
        lax.all_gather(grad_out, "col", axis=0, tiled=True),
    )
    gate_sum, up_sum, grad_hidden = (
        lax.psum(
            jnp.dot(tok_all, gate_weight, preferred_element_type=jnp.float32).astype(jnp.bfloat16),
            "row",
        ).astype(jnp.float32),
        lax.psum(
            jnp.dot(tok_all, up_weight, preferred_element_type=jnp.float32).astype(jnp.bfloat16),
            "row",
        ).astype(jnp.float32),
        lax.psum(contract_last(grad_all, down_weight).astype(jnp.bfloat16), "row").astype(
            jnp.float32
        ),
    )
    hidden, grad_gate, grad_up = gated_grads(gate_sum, up_sum, grad_hidden)
    acc_gate = contract_first(tok_all, grad_gate)
    acc_up = contract_first(tok_all, grad_up)
    acc_down = contract_first(hidden, grad_all)
    partial_grad = contract_last(grad_gate, gate_weight) + contract_last(grad_up, up_weight)
    grad_tokens = lax.psum_scatter(
        partial_grad.astype(jnp.bfloat16), "col", scatter_dimension=0, tiled=True
    )
    return (
        grad_tokens,
        acc_gate.astype(jnp.bfloat16),
        acc_up.astype(jnp.bfloat16),
        acc_down.astype(jnp.bfloat16),
    )


def solution(mesh):
    return jax.shard_map(
        body,
        mesh=mesh,
        in_specs=(
            P("col", "row"),
            P("col", "row"),
            P("row", "col"),
            P("row", "col"),
            P("col", "row"),
        ),
        out_specs=(P("col", "row"), P("row", "col"), P("row", "col"), P("col", "row")),
        check_vma=False,
    )
```

profile of v0, /device:TPU:0, one launch (start us, length us, event | category | flops | bytes accessed | tf_op | source)
XLA Modules:
  0.0 188.0 jit_solution(11670191383653160460)
XLA Ops:
  7.2 0.0 all-reduce.3.cloned.1.call-start
  7.2 16.5 %all_gather.7 = bf16[192,1024]{1,0:T(8,128)(2,1)S(1)} all-gather(bf16[48,1024]{1,0:T(8,128)(2,1)} %param.5), channel_id=1, replica_groups=mesh['row'=8,'col'=4] {'col'}, dimensions={0}, use_global_device_ids=true | all-gather | bytes 491520 | tf_op jit(solution)/shard_map/all_gather | solution.py:31
  23.7 15.8 %all_gather.6 = bf16[192,1024]{1,0:T(8,128)(2,1)S(1)} all-gather(bf16[48,1024]{1,0:T(8,128)(2,1)} %param.6), channel_id=1, replica_groups=mesh['row'=8,'col'=4] {'col'}, dimensions={0}, use_global_device_ids=true | all-gather | bytes 491520 | tf_op jit(solution)/shard_map/all_gather | solution.py:32
  39.4 0.0 copy-start.4
  39.4 0.0 slice-start
  39.4 5.9 %convolution_convert_fusion.4 = bf16[192,3584]{1,0:T(8,128)(2,1)} fusion(bf16[192,1024]{1,0:T(8,128)(2,1)S(1)} %all_gather.7, bf16[1024,3584]{1,0:T(8,128)(2,1)} %param.8), kind=kOutput, calls=%fused_computation.6 | convolution fusion | flops 1409974272 | bytes 9109504 | tf_op jit(solution)/shard_map/dot_general | solution.py:40
  45.4 0.0 copy-done.4
  45.4 0.0 slice-start.1
  45.4 2.7 %convolution_convert_fusion.3 = bf16[192,3584]{1,0:T(8,128)(2,1)} fusion(bf16[192,1024]{1,0:T(8,128)(2,1)S(1)} %all_gather.7, bf16[1024,3584]{1,0:T(8,128)(2,1)S(1)} %copy-done.4), kind=kOutput, calls=%fused_computation.5 | convolution fusion | flops 1409974272 | bytes 9109504 | tf_op jit(solution)/shard_map/dot_general | solution.py:36
  48.1 0.0 slice-done
  48.1 0.0 slice-done.1
  48.1 3.6 %convolution_convert_fusion.5 = bf16[192,3584]{1,0:T(8,128)(2,1)} fusion(bf16[192,1024]{1,0:T(8,128)(2,1)S(1)} %all_gather.6, bf16[3584,1024]{1,0:T(8,128)(2,1)S(1)} %bitcast.18), kind=kOutput, calls=%fused_computation.7 | convolution fusion | flops 1409974272 | bytes 9109504 | tf_op jit(solution)/shard_map/dot_general | solution.py:14
  51.7 0.0 all-reduce.3.cloned.1.call-update
  51.7 0.2 reduce-scatter.2.cloned.1.call-start
  51.9 81.2 %all-reduce.3.cloned.1.call-done = (bf16[192,3584]{1,0:T(8,128)(2,1)}, bf16[192,3584]{1,0:T(8,128)(2,1)}, bf16[192,3584]{1,0:T(8,128)(2,1)}) async-done(((bf16[192,3584]{1,0:T(8,128)(2,1)}, bf16[192,3584]{1,0:T(8,128)(2,1)}, bf16[192,3584]{1,0:T(8,128)(2,1)}), (bf16[192,3584]{1,0:T(8,128)(2,1)}, bf16[192,3584]{1,0:T(8,128)(2,1)}, bf16[192,3584]{1,0:T(8,128)(2,1)})) %all-reduce.3.cloned.1.call-update) | async-done | bytes 4128784 | tf_op jit(solution)/shard_map/psum | solution.py:39
  133.2 0.0 copy-start
  133.2 0.0 copy-start.1
  133.2 0.0 copy-start.3
  133.2 7.0 %fusion.1 = bf16[1024,3584]{0,1:T(8,128)(2,1)} fusion(bf16[192,1024]{1,0:T(8,128)(2,1)S(1)} %all_gather.7, bf16[192,3584]{1,0:T(8,128)(2,1)} %get-tuple-element.10, bf16[192,3584]{1,0:T(8,128)(2,1)} %get-tuple-element.9), kind=kOutput, calls=%fused_computation.4 | convolution fusion | flops 1418461184 | bytes 10485760 | tf_op jit(solution)/shard_map/dot_general | solution.py:8
  140.2 0.0 copy-done
  140.2 0.0 copy-done.1
  140.2 0.0 copy-done.3
  140.2 0.0 slice-start.2
  140.3 1.2 fusion.4
  141.5 0.0 slice-start.3
  141.5 5.7 %fusion.18 = f32[192,1024]{1,0:T(8,128)S(1)} fusion(bf16[192,3584]{1,0:T(8,128)(2,1)S(1)} %fusion.4, bf16[1024,3584]{1,0:T(8,128)(2,1)} %param.7), kind=kOutput, calls=%fused_computation.28 | convolution fusion | flops 1409286144 | bytes 9502720 | tf_op jit(solution)/shard_map/dot_general | solution.py:14
  147.2 0.0 slice-done.2
  147.3 0.0 slice-done.3
  147.3 3.4 %fusion.14 = bf16[192,1024]{1,0:T(8,128)(2,1)} fusion(f32[192,1024]{1,0:T(8,128)S(1)} %fusion.18, bf16[1024,3584]{1,0:T(8,128)(2,1)S(1)} %bitcast.20, bf16[192,3584]{1,0:T(8,128)(2,1)S(1)} %copy-done.1, bf16[192,3584]{1,0:T(8,128)(2,1)S(1)} %copy-done.3), kind=kOutput, calls=%fused_computation.26 | convolution fusion | flops 1415184384 | bytes 11272192 | tf_op jit(solution)/shard_map/dot_general | solution.py:14
  150.6 0.0 reduce-scatter.2.cloned.1.call-update
  150.7 5.2 %fusion = bf16[1024,3584]{0,1:T(8,128)(2,1)} fusion(bf16[192,3584]{1,0:T(8,128)(2,1)S(1)} %fusion.4, bf16[192,1024]{1,0:T(8,128)(2,1)S(1)} %all_gather.7), kind=kOutput, calls=%fused_computation.3 | convolution fusion | flops 1412956160 | bytes 9109504 | tf_op jit(solution)/shard_map/dot_general | solution.py:8
  155.8 10.0 %copy.9 = bf16[1024,3584]{1,0:T(8,128)(2,1)} copy(bf16[1024,3584]{0,1:T(8,128)(2,1)} %fusion) | data formatting | bytes 14680064
  165.8 0.0 copy-start.2
  165.8 10.0 %copy.10 = bf16[1024,3584]{1,0:T(8,128)(2,1)} copy(bf16[1024,3584]{0,1:T(8,128)(2,1)} %fusion.1) | data formatting | bytes 14680064
  175.8 0.0 copy-done.2
  175.8 5.3 %convolution_convert_fusion = bf16[3584,1024]{1,0:T(8,128)(2,1)} fusion(bf16[192,1024]{1,0:T(8,128)(2,1)S(1)} %all_gather.6, bf16[192,3584]{1,0:T(8,128)(2,1)S(1)} %copy-done, bf16[192,3584]{1,0:T(8,128)(2,1)S(1)} %copy-done.2), kind=kOutput, calls=%fused_computation | convolution fusion | flops 1418461184 | bytes 10485760 | tf_op jit(solution)/shard_map/dot_general | solution.py:8
  181.1 0.0 reduce-scatter.2.cloned.1.call-done
  (2 shorter events, 0.0 us)
Async XLA Ops:
  7.2 126.0 %all-reduce.3.cloned.1.call-start = ((), (), s32[]{:S(2)}) async-start(), calls=%async_computation.2 | async-start | bytes 8257536 | tf_op jit(solution)/shard_map/psum | solution.py:39
  39.4 5.9 %copy-start.4 = (bf16[1024,3584]{1,0:T(8,128)(2,1)S(1)}, bf16[1024,3584]{1,0:T(8,128)(2,1)}, u32[]{:S(2)}) copy-start(bf16[1024,3584]{1,0:T(8,128)(2,1)} %param.7) | copy-start | bytes 22020100
  39.4 8.6 %slice-start = ((s8[7340032]{0:T(1024)(128)(4,1)}), s8[4194304]{0:T(1024)(128)(4,1)S(1)}, s32[]{:S(2)}) async-start(s8[7340032]{0:T(1024)(128)(4,1)} %bitcast.17), calls=%async_computation.3 | async-start | bytes 8388608
  45.4 2.7 %slice-start.1 = ((s8[7340032]{0:T(1024)(128)(4,1)}), s8[3145728]{0:T(1024)(128)(4,1)S(1)}, s32[]{:S(2)}) async-start(s8[7340032]{0:T(1024)(128)(4,1)} %bitcast.17), calls=%async_computation.4 | async-start | bytes 6291456
  51.7 129.4 %reduce-scatter.2.cloned.1.call-start = ((), (), s32[]{:S(2)}) async-start(), calls=%async_computation.1 | async-start | bytes 491520 | tf_op jit(solution)/shard_map/reduce_scatter | solution.py:52
  133.2 7.1 %copy-start = (bf16[192,3584]{1,0:T(8,128)(2,1)S(1)}, bf16[192,3584]{1,0:T(8,128)(2,1)}, u32[]{:S(2)}) copy-start(bf16[192,3584]{1,0:T(8,128)(2,1)} %get-tuple-element.8) | copy-start | bytes 4128772
  133.2 7.1 %copy-start.1 = (bf16[192,3584]{1,0:T(8,128)(2,1)S(1)}, bf16[192,3584]{1,0:T(8,128)(2,1)}, u32[]{:S(2)}) copy-start(bf16[192,3584]{1,0:T(8,128)(2,1)} %get-tuple-element.10) | copy-start | bytes 4128772
  133.2 7.1 %copy-start.3 = (bf16[192,3584]{1,0:T(8,128)(2,1)S(1)}, bf16[192,3584]{1,0:T(8,128)(2,1)}, u32[]{:S(2)}) copy-start(bf16[192,3584]{1,0:T(8,128)(2,1)} %get-tuple-element.9) | copy-start | bytes 4128772
  140.2 7.0 %slice-start.2 = ((s8[7340032]{0:T(1024)(128)(4,1)}), s8[4194304]{0:T(1024)(128)(4,1)S(1)}, s32[]{:S(2)}) async-start(s8[7340032]{0:T(1024)(128)(4,1)} %bitcast.19), calls=%async_computation.5 | async-start | bytes 8388608
  141.5 5.8 %slice-start.3 = ((s8[7340032]{0:T(1024)(128)(4,1)}), s8[3145728]{0:T(1024)(128)(4,1)S(1)}, s32[]{:S(2)}) async-start(s8[7340032]{0:T(1024)(128)(4,1)} %bitcast.19), calls=%async_computation.6 | async-start | bytes 6291456
  165.8 10.0 %copy-start.2 = (bf16[192,3584]{1,0:T(8,128)(2,1)S(1)}, bf16[192,3584]{1,0:T(8,128)(2,1)}, u32[]{:S(2)}) copy-start(bf16[192,3584]{1,0:T(8,128)(2,1)} %get-tuple-element.10) | copy-start | bytes 4128772
Sparse Core Ops, SparseCore 0:
  51.8 81.3 all-reduce.2
  150.8 20.8 reduce-scatter.1
where the time goes:
time: 189 us; the launch traced here: 188 us
  waiting for transfers between devices  81.3 us (43%)
  matrix products  38.8 us (21%)
  blocking collectives  32.2 us (17%)
  local copies, waits for them, and re-layouts  20.1 us (11%)
  between operations  14.1 us (7%)
    psum x1, waiting for transfers between devices, body(): lax.psum(jnp.dot(tok_all, up_weight, preferred_element_type=jnp.float32)....  81.2 us
    unnamed x20, local copies, waits for them, and re-layouts  20.1 us
    dot_general x3, matrix products, contract_first(): lax.dot_general(left, right, (((0,), (0,)), ((), ())), preferred_element_...  17.5 us
    all_gather x1, blocking collectives, body(): lax.all_gather(tokens, 'col', axis=0, tiled=True)  16.5 us
    all_gather x1, blocking collectives, body(): lax.all_gather(grad_out, 'col', axis=0, tiled=True)  15.8 us
    dot_general x3, matrix products, contract_last(): lax.dot_general(left, right, (((1,), (1,)), ((), ())), preferred_element_...  12.7 us
    dot_general x1, matrix products, body(): jnp.dot(tok_all, up_weight, preferred_element_type=jnp.float32)  5.91 us
  transfers between devices with their start and end apart: 2, of which 1 were waited for; matrix products, arithmetic and copies ran while one was open for 16% of the time, Pallas kernels for 0%

commit v1 on v0

--- a/solution.py
+++ b/solution.py
@@ -2,6 +2,31 @@
 import jax.numpy as jnp
 from jax import lax
 from jax.sharding import PartitionSpec as P
+
+
+def state_wires(buf, on_dim):
+    buf = jnp.moveaxis(buf, 0, on_dim)
+    tmp = buf.shape
+    return buf.reshape(*tmp[:on_dim], tmp[on_dim] * tmp[on_dim + 1], *tmp[on_dim + 2 :])
+
+
+def tails_find(t0, dev_axis):
+    everything = t0[None]
+    chips = lax.axis_size(dev_axis)
+    for m in range(chips.bit_length() - 1):
+        then = 1 << m
+        x_next = lax.ppermute(
+            everything, dev_axis, list(map(lambda rr: (rr, rr ^ then), range(chips)))
+        )
+        long_array = jnp.stack([everything, x_next], 0)
+        k_now = lax.axis_index(dev_axis) >> m & 1
+        everything = jnp.where(k_now == 0, long_array, long_array[::-1]).reshape(-1, *t0.shape)
+    return everything
+
+
+def map_compute(mat, payload, k_dim):
+    extra = tails_find(mat, payload)
+    return state_wires(extra, k_dim)
 
 
 def contract_first(left, right):
@@ -29,7 +54,7 @@
 def body(tokens, grad_out, gate_weight, up_weight, down_weight):
     tok_all, grad_all = (
         lax.all_gather(tokens, "col", axis=0, tiled=True),
-        lax.all_gather(grad_out, "col", axis=0, tiled=True),
+        map_compute(grad_out, "col", 0),
     )
     gate_sum, up_sum, grad_hidden = (
         lax.psum(

time: 189 us -> 183 us (0.968)
  blocking collectives: 32.2 us -> 14.8 us
  matrix products: 38.8 us -> 44.9 us
  starting transfers between devices: 0.26 us -> 4.13 us
    all_gather x1 -> x0, blocking collectives: 15.8 us -> none  [body(): lax.all_gather(grad_out, 'col', axis=0, tiled=True)]
    ppermute x0 -> x2, starting transfers between devices: none -> 3.87 us  [tails_find(): lax.ppermute(everything, dev_axis, list(map(lambda rr: (rr, rr ^ then), r...]
    dot_general x3, matrix products: 12.7 us -> 15.8 us  [contract_last(): lax.dot_general(left, right, (((1,), (1,)), ((), ())), preferred_element_...]
    dot_general x1, matrix products: 2.7 us -> 5.76 us  [body(): jnp.dot(tok_all, gate_weight, preferred_element_type=jnp.float32)]
    ppermute x0 -> x2, waiting for transfers between devices: none -> 2.23 us  [tails_find(): lax.ppermute(everything, dev_axis, list(map(lambda rr: (rr, rr ^ then), r...]
    unnamed x20 -> x16, local copies, waits for them, and re-layouts: 20.1 us -> 20.1 us
  transfers between devices with their start and end apart: 2 -> 4, of which waited for: 1 -> 2; matrix products, arithmetic and copies ran while one was open for 16% -> 23% of each run, Pallas kernels for 0% -> 0%
where the time goes in v1:
time: 183 us; the launch traced here: 182 us
  waiting for transfers between devices  82.6 us (45%)
  matrix products  44.9 us (25%)
  local copies, waits for them, and re-layouts  20.1 us (11%)
  blocking collectives  14.8 us (8%)
  between operations  14.1 us (8%)
  starting transfers between devices  4.13 us (2%)
    psum x1, waiting for transfers between devices, body(): lax.psum(jnp.dot(tok_all, up_weight, preferred_element_type=jnp.float32)....  80.4 us
    unnamed x16, local copies, waits for them, and re-layouts  20.1 us
    dot_general x3, matrix products, contract_first(): lax.dot_general(left, right, (((0,), (0,)), ((), ())), preferred_element_...  17.5 us
    dot_general x3, matrix products, contract_last(): lax.dot_general(left, right, (((1,), (1,)), ((), ())), preferred_element_...  15.8 us
    all_gather x1, blocking collectives, body(): lax.all_gather(tokens, 'col', axis=0, tiled=True)  14.8 us
    dot_general x1, matrix products, body(): jnp.dot(tok_all, up_weight, preferred_element_type=jnp.float32)  5.8 us
    dot_general x1, matrix products, body(): jnp.dot(tok_all, gate_weight, preferred_element_type=jnp.float32)  5.76 us
    ppermute x2, starting transfers between devices, tails_find(): lax.ppermute(everything, dev_axis, list(map(lambda rr: (rr, rr ^ then), r...  3.87 us
  transfers between devices with their start and end apart: 4, of which 2 were waited for; matrix products, arithmetic and copies ran while one was open for 23% of the time, Pallas kernels for 0%

profile of v1, /device:TPU:0, one launch (start us, length us, event | category | flops | bytes accessed | tf_op | source)
XLA Modules:
  0.0 182.0 jit_solution(12897079581404501808)
XLA Ops:
  7.2 0.0 all-reduce.3.cloned.1.call-start
  7.2 3.1 %collective-permute-start = (bf16[1,48,1024]{2,1,0:T(8,128)(2,1)}, bf16[1,48,1024]{2,1,0:T(8,128)(2,1)S(1)}, u32[]{:S(2)}, u32[]{:S(2)}) collective-permute-start(bf16[1,48,1024]{2,1,0:T(8,128)(2,1)} %bitcast.29), channel_id=1, source_target_pairs={{0,1},{1,0},{2,3},{3,2},{4,5},{5,4},{6,7},{7,6},{8,9},{9,8},{10,11... | collective-permute-start | bytes 294920 | tf_op jit(solution)/shard_map/ppermute | solution.py:18
  10.3 14.8 %all_gather.3 = bf16[192,1024]{1,0:T(8,128)(2,1)S(1)} all-gather(bf16[48,1024]{1,0:T(8,128)(2,1)} %param.5), channel_id=1, replica_groups=mesh['row'=8,'col'=4] {'col'}, dimensions={0}, use_global_device_ids=true | all-gather | bytes 491520 | tf_op jit(solution)/shard_map/all_gather | solution.py:56
  25.1 0.0 copy-start.4
  25.1 5.8 %convolution_convert_fusion.4 = bf16[192,3584]{1,0:T(8,128)(2,1)} fusion(bf16[192,1024]{1,0:T(8,128)(2,1)S(1)} %all_gather.3, bf16[1024,3584]{1,0:T(8,128)(2,1)} %param.8), kind=kOutput, calls=%fused_computation.6 | convolution fusion | flops 1409974272 | bytes 9109504 | tf_op jit(solution)/shard_map/dot_general | solution.py:65
  30.9 0.0 collective-permute-done
  30.9 0.0 copy-done.4
  31.0 0.8 collective-permute-start.1
  31.7 5.8 %convolution_convert_fusion.3 = bf16[192,3584]{1,0:T(8,128)(2,1)} fusion(bf16[192,1024]{1,0:T(8,128)(2,1)S(1)} %all_gather.3, bf16[1024,3584]{1,0:T(8,128)(2,1)} %param.7), kind=kOutput, calls=%fused_computation.5 | convolution fusion | flops 1409974272 | bytes 9109504 | tf_op jit(solution)/shard_map/dot_general | solution.py:61
  37.5 2.2 %collective-permute-done.1 = bf16[2,48,1024]{2,1,0:T(8,128)(2,1)S(1)} collective-permute-done((bf16[2,48,1024]{2,1,0:T(8,128)(2,1)S(1)}, bf16[2,48,1024]{2,1,0:T(8,128)(2,1)S(1)}, u32[]{:S(2)}, u32[]{:S(2)}) %collective-permute-start.1) | collective-permute-done | bytes 196640 | tf_op jit(solution)/shard_map/ppermute | solution.py:18
  39.8 0.1 reverse_select_fusion
  39.8 6.7 %convolution_convert_fusion.5 = bf16[192,3584]{1,0:T(8,128)(2,1)} fusion(bf16[192,1024]{1,0:T(8,128)(2,1)S(1)} %bitcast.26, bf16[3584,1024]{1,0:T(8,128)(2,1)} %param.9), kind=kOutput, calls=%fused_computation.7 | convolution fusion | flops 1409974272 | bytes 9109504 | tf_op jit(solution)/shard_map/dot_general | solution.py:39
  46.6 0.0 all-reduce.3.cloned.1.call-update
  46.6 0.2 reduce-scatter.2.cloned.1.call-start
  46.8 80.4 %all-reduce.3.cloned.1.call-done = (bf16[192,3584]{1,0:T(8,128)(2,1)}, bf16[192,3584]{1,0:T(8,128)(2,1)}, bf16[192,3584]{1,0:T(8,128)(2,1)}) async-done(((bf16[192,3584]{1,0:T(8,128)(2,1)}, bf16[192,3584]{1,0:T(8,128)(2,1)}, bf16[192,3584]{1,0:T(8,128)(2,1)}), (bf16[192,3584]{1,0:T(8,128)(2,1)}, bf16[192,3584]{1,0:T(8,128)(2,1)}, bf16[192,3584]{1,0:T(8,128)(2,1)})) %all-reduce.3.cloned.1.call-update) | async-done | bytes 4128784 | tf_op jit(solution)/shard_map/psum | solution.py:64
  127.2 0.0 copy-start
  127.2 0.0 copy-start.1
  127.2 0.0 copy-start.3
  127.2 7.1 %fusion.1 = bf16[1024,3584]{0,1:T(8,128)(2,1)} fusion(bf16[192,1024]{1,0:T(8,128)(2,1)S(1)} %all_gather.3, bf16[192,3584]{1,0:T(8,128)(2,1)} %get-tuple-element.10, bf16[192,3584]{1,0:T(8,128)(2,1)} %get-tuple-element.9), kind=kOutput, calls=%fused_computation.4 | convolution fusion | flops 1418461184 | bytes 10485760 | tf_op jit(solution)/shard_map/dot_general | solution.py:33
  134.2 0.0 copy-done
  134.2 0.0 copy-done.1
  134.2 0.0 copy-done.3
  134.2 0.0 slice-start
  134.3 1.2 fusion.4
  135.5 0.0 slice-start.1
  135.5 5.7 %fusion.20 = f32[192,1024]{1,0:T(8,128)S(1)} fusion(bf16[192,3584]{1,0:T(8,128)(2,1)S(1)} %fusion.4, bf16[1024,3584]{1,0:T(8,128)(2,1)} %param.7), kind=kOutput, calls=%fused_computation.34 | convolution fusion | flops 1409286144 | bytes 9502720 | tf_op jit(solution)/shard_map/dot_general | solution.py:39
  141.2 0.0 slice-done
  141.2 0.0 slice-done.1
  141.3 3.3 %fusion.14 = bf16[192,1024]{1,0:T(8,128)(2,1)} fusion(f32[192,1024]{1,0:T(8,128)S(1)} %fusion.20, bf16[1024,3584]{1,0:T(8,128)(2,1)S(1)} %bitcast.33, bf16[192,3584]{1,0:T(8,128)(2,1)S(1)} %copy-done.1, bf16[192,3584]{1,0:T(8,128)(2,1)S(1)} %copy-done.3), kind=kOutput, calls=%fused_computation.26 | convolution fusion | flops 1415184384 | bytes 11272192 | tf_op jit(solution)/shard_map/dot_general | solution.py:39
  144.6 0.0 reduce-scatter.2.cloned.1.call-update
  144.6 5.2 %fusion = bf16[1024,3584]{0,1:T(8,128)(2,1)} fusion(bf16[192,3584]{1,0:T(8,128)(2,1)S(1)} %fusion.4, bf16[192,1024]{1,0:T(8,128)(2,1)S(1)} %all_gather.3), kind=kOutput, calls=%fused_computation.3 | convolution fusion | flops 1412956160 | bytes 9109504 | tf_op jit(solution)/shard_map/dot_general | solution.py:33
  149.8 10.0 %copy.9 = bf16[1024,3584]{1,0:T(8,128)(2,1)} copy(bf16[1024,3584]{0,1:T(8,128)(2,1)} %fusion) | data formatting | bytes 14680064
  159.8 0.0 copy-start.2
  159.8 10.0 %copy.10 = bf16[1024,3584]{1,0:T(8,128)(2,1)} copy(bf16[1024,3584]{0,1:T(8,128)(2,1)} %fusion.1) | data formatting | bytes 14680064
  169.8 0.0 copy-done.2
  169.8 5.3 %convolution_convert_fusion = bf16[3584,1024]{1,0:T(8,128)(2,1)} fusion(bf16[192,1024]{1,0:T(8,128)(2,1)S(1)} %bitcast.27, bf16[192,3584]{1,0:T(8,128)(2,1)S(1)} %copy-done, bf16[192,3584]{1,0:T(8,128)(2,1)S(1)} %copy-done.2), kind=kOutput, calls=%fused_computation | convolution fusion | flops 1418461184 | bytes 10485760 | tf_op jit(solution)/shard_map/dot_general | solution.py:33
  175.1 0.0 reduce-scatter.2.cloned.1.call-done
  (4 shorter events, 0.1 us)
Async XLA Ops:
  7.2 120.0 %all-reduce.3.cloned.1.call-start = ((), (), s32[]{:S(2)}) async-start(), calls=%async_computation.2 | async-start | bytes 8257536 | tf_op jit(solution)/shard_map/psum | solution.py:64
  7.2 23.7 %collective-permute-start = (bf16[1,48,1024]{2,1,0:T(8,128)(2,1)}, bf16[1,48,1024]{2,1,0:T(8,128)(2,1)S(1)}, u32[]{:S(2)}, u32[]{:S(2)}) collective-permute-start(bf16[1,48,1024]{2,1,0:T(8,128)(2,1)} %bitcast.29), channel_id=1, source_target_pairs={{0,1},{1,0},{2,3},{3,2},{4,5},{5,4},{6,7},{7,6},{8,9},{9,8},{10,11... | collective-permute-start | bytes 294920 | tf_op jit(solution)/shard_map/ppermute | solution.py:18
  25.1 5.8 %copy-start.4 = (bf16[48,1024]{1,0:T(8,128)(2,1)S(1)}, bf16[48,1024]{1,0:T(8,128)(2,1)}, u32[]{:S(2)}) copy-start(bf16[48,1024]{1,0:T(8,128)(2,1)} %param.6) | copy-start | bytes 294916
  31.0 8.7 %collective-permute-start.1 = (bf16[2,48,1024]{2,1,0:T(8,128)(2,1)S(1)}, bf16[2,48,1024]{2,1,0:T(8,128)(2,1)S(1)}, u32[]{:S(2)}, u32[]{:S(2)}) collective-permute-start(bf16[2,48,1024]{2,1,0:T(8,128)(2,1)S(1)} %get-tuple-element.12), channel_id=1, source_target_pairs={{0,2},{1,3},{2,0},{3,1},{4,6},{5,7},{6,4},{7,5},{8,10},{9,11},{10,... | collective-permute-start | bytes 589832 | tf_op jit(solution)/shard_map/ppermute | solution.py:18
  46.6 128.5 %reduce-scatter.2.cloned.1.call-start = ((), (), s32[]{:S(2)}) async-start(), calls=%async_computation.1 | async-start | bytes 491520 | tf_op jit(solution)/shard_map/reduce_scatter | solution.py:77
  127.2 7.1 %copy-start = (bf16[192,3584]{1,0:T(8,128)(2,1)S(1)}, bf16[192,3584]{1,0:T(8,128)(2,1)}, u32[]{:S(2)}) copy-start(bf16[192,3584]{1,0:T(8,128)(2,1)} %get-tuple-element.8) | copy-start | bytes 4128772
  127.2 7.1 %copy-start.1 = (bf16[192,3584]{1,0:T(8,128)(2,1)S(1)}, bf16[192,3584]{1,0:T(8,128)(2,1)}, u32[]{:S(2)}) copy-start(bf16[192,3584]{1,0:T(8,128)(2,1)} %get-tuple-element.10) | copy-start | bytes 4128772
  127.2 7.1 %copy-start.3 = (bf16[192,3584]{1,0:T(8,128)(2,1)S(1)}, bf16[192,3584]{1,0:T(8,128)(2,1)}, u32[]{:S(2)}) copy-start(bf16[192,3584]{1,0:T(8,128)(2,1)} %get-tuple-element.9) | copy-start | bytes 4128772
  134.2 7.0 %slice-start = ((s8[7340032]{0:T(1024)(128)(4,1)}), s8[4194304]{0:T(1024)(128)(4,1)S(1)}, s32[]{:S(2)}) async-start(s8[7340032]{0:T(1024)(128)(4,1)} %bitcast.32), calls=%async_computation.3 | async-start | bytes 8388608
  135.5 5.8 %slice-start.1 = ((s8[7340032]{0:T(1024)(128)(4,1)}), s8[3145728]{0:T(1024)(128)(4,1)S(1)}, s32[]{:S(2)}) async-start(s8[7340032]{0:T(1024)(128)(4,1)} %bitcast.32), calls=%async_computation.4 | async-start | bytes 6291456
  159.8 10.0 %copy-start.2 = (bf16[192,3584]{1,0:T(8,128)(2,1)S(1)}, bf16[192,3584]{1,0:T(8,128)(2,1)}, u32[]{:S(2)}) copy-start(bf16[192,3584]{1,0:T(8,128)(2,1)} %get-tuple-element.10) | copy-start | bytes 4128772
Sparse Core Ops, SparseCore 0:
  46.7 80.4 all-reduce.2
  144.8 20.8 reduce-scatter.1
